TPU v7x, 512 devices: a whole 4x4x16 slice. The times are simulated.
512 devices in a mesh: dp: 16 (over z), owner: 32 (over x, y, core).
Axes of the slice: x: 4, y: 4, z: 16, core: 2. Of those that a mesh axis runs over, the one named last changes fastest.
Arguments:
- tokens: bfloat16 [65536, 8192], P(('dp', 'owner')), may hold values from -6 to 6
- residual: bfloat16 [65536, 8192], P(('dp', 'owner')), may hold values from -6 to 6
- token_adapter_index: int32 [65536, 1], P(('dp', 'owner')), may hold values from 0 to 31; in each aligned block of 128 rows (0 to 127, 128 to 255, ...) at most 6 rows name the same one
- adapter_down_weight: bfloat16 [32, 64, 8192], P('owner', None, 'dp'), may hold values from -0.0625 to 0.0625
- adapter_up_weight: bfloat16 [32, 64, 8192], P('owner', None, 'dp'), may hold values from -0.75 to 0.75
- down_moment_first: bfloat16 [32, 64, 8192], P('owner', None, 'dp'), may hold values from -270 to 270
- down_moment_second: bfloat16 [32, 64, 8192], P('owner', None, 'dp'), may hold values from 816 to 24576
- up_moment_first: bfloat16 [32, 64, 8192], P('owner', None, 'dp'), may hold values from -27.125 to 27.125
- up_moment_second: bfloat16 [32, 64, 8192], P('owner', None, 'dp'), may hold values from 6.125 to 204
Outputs:
- down_update: float32 [32, 64, 8192], P('owner', None, 'dp')
- up_update: float32 [32, 64, 8192], P('owner', None, 'dp')
- token_loss: float32 [65536], P(('dp', 'owner'))
Inputs may be any that keep to these rules, and one draw needn't show every extreme that they name: `token_adapter_index`: of the 128 rows of one device, at most 6 name one adapter, and in some devices one adapter is named by exactly 6.
All inputs are finite; a program needn't handle non-finite values.
Results may differ from a plain program's by a relative error of at most 0.0091.
Values may be sent and summed in bfloat16 or wider, within the bound.
No kernel may reach another device: no remote copies, remote signals or barrier semaphores. Data moves between devices by JAX's collectives and lax.ppermute only.
A program may use at most 128 MiB of HBM per device.

v0:
```python
import jax
import jax.numpy as jnp
from jax import lax
from jax.sharding import PartitionSpec as P

adapter_scale = 0.5
adam_eps = 1e-08


def adam_update(grad, first, second):
    first_new = 0.9 * first.astype(jnp.float32) + 0.1 * grad
    second_new = 0.95 * second.astype(jnp.float32) + 0.05 * grad * grad
    return first_new / (jnp.sqrt(second_new) + adam_eps)


def body(
    tokens,
    residual,
    token_adapter_index,
    adapter_down_weight,
    adapter_up_weight,
    down_moment_first,
    down_moment_second,
    up_moment_first,
    up_moment_second,
):
    owner_index = lax.axis_size("owner")
    tok_rows = tokens.shape[0]
    model_width_value = tokens.shape[1]
    column_span = adapter_down_weight.shape[2]
    slot_capacity = max(2, 3 * tok_rows // (2 * owner_index))
    route_ids = token_adapter_index[:, 0]
    member = (route_ids[:, None] == jnp.arange(owner_index, dtype=jnp.int32)[None, :]).astype(
        jnp.int32
    )
    before = jnp.cumsum(member, axis=0) - member
    within = jnp.sum(before * member, axis=1)
    target = route_ids * slot_capacity + within
    dispatch = (
        jnp.arange(owner_index * slot_capacity, dtype=jnp.int32)[:, None] == target[None, :]
    ).astype(jnp.bfloat16)

    def placed_rows(row_block):
        return jnp.dot(dispatch, row_block, preferred_element_type=jnp.float32).astype(jnp.bfloat16)

    down_full, up_weight_whole = (
        lax.all_gather(adapter_down_weight, "dp", axis=2, tiled=True),
        lax.all_gather(adapter_up_weight, "dp", axis=2, tiled=True),
    )
    down_full = down_full[0]
    up_weight_whole = up_weight_whole[0]

    def spread(row_block):
        return placed_rows(row_block).reshape(owner_index, slot_capacity, model_width_value)

    arrived = lax.all_to_all(
        spread(tokens), "owner", split_axis=0, concat_axis=0, tiled=True
    ).reshape(owner_index * slot_capacity, model_width_value)
    hidden_state = lax.dot_general(
        arrived, down_full, (((1,), (1,)), ((), ())), preferred_element_type=jnp.float32
    ).astype(jnp.bfloat16)
    adapter_output = (
        adapter_scale * jnp.dot(hidden_state, up_weight_whole, preferred_element_type=jnp.float32)
    ).astype(jnp.bfloat16)
    hidden_state, adapter_output = (hidden_state, adapter_output)
    returned = lax.all_to_all(
        adapter_output.reshape(owner_index, slot_capacity, model_width_value),
        "owner",
        split_axis=0,
        concat_axis=0,
        tiled=True,
    )
    returned = returned.reshape(owner_index * slot_capacity, model_width_value)
    adapter_home_index = lax.dot_general(
        dispatch, returned, (((0,), (0,)), ((), ())), preferred_element_type=jnp.float32
    )
    shifted_index = residual.astype(jnp.float32) + adapter_home_index
    token_loss = jnp.mean(0.5 * shifted_index * shifted_index, axis=1)
    output_gradient = lax.all_to_all(
        spread(shifted_index.astype(jnp.bfloat16)), "owner", split_axis=0, concat_axis=0, tiled=True
    )
    output_gradient = output_gradient.reshape(owner_index * slot_capacity, model_width_value)
    up_gradient = adapter_scale * lax.dot_general(
        hidden_state, output_gradient, (((0,), (0,)), ((), ())), preferred_element_type=jnp.float32
    )
    hidden_gradient = (
        adapter_scale
        * lax.dot_general(
            output_gradient,
            up_weight_whole,
            (((1,), (1,)), ((), ())),
            preferred_element_type=jnp.float32,
        )
    ).astype(jnp.bfloat16)
    down_grad = lax.dot_general(
        hidden_gradient, arrived, (((0,), (0,)), ((), ())), preferred_element_type=jnp.float32
    )
    summed_down, summed_up = lax.psum((down_grad, up_gradient), "dp")
    offset = lax.axis_index("dp") * column_span
    down_share = lax.dynamic_slice_in_dim(summed_down, offset, column_span, 1)
    up_share = lax.dynamic_slice_in_dim(summed_up, offset, column_span, 1)
    down_update = adam_update(down_share, down_moment_first[0], down_moment_second[0])
    up_update = adam_update(up_share, up_moment_first[0], up_moment_second[0])
    return (down_update[None], up_update[None], token_loss)


def solution(mesh):
    return jax.shard_map(
        body,
        mesh=mesh,
        in_specs=(
            P(("dp", "owner"), None),
            P(("dp", "owner"), None),
            P(("dp", "owner"), None),
            P("owner", None, "dp"),
            P("owner", None, "dp"),
            P("owner", None, "dp"),
            P("owner", None, "dp"),
            P("owner", None, "dp"),
            P("owner", None, "dp"),
        ),
        out_specs=(P("owner", None, "dp"), P("owner", None, "dp"), P(("dp", "owner"))),
        check_vma=False,
    )
```

profile of v0, /device:TPU:6, one launch (start us, length us, event | category | flops | bytes accessed | tf_op | source)
XLA Modules:
  0.0 467.8 jit_solution(18413843679098739913)
XLA Ops:
  7.2 0.0 all-gather.3.cloned.1.call-start
  7.2 0.7 all-gather.3.cloned.1.call-update
  7.9 0.7 fusion.19
  8.7 0.2 reduce_window_sum.11
  8.8 0.8 select_reduce_fusion
  9.7 0.7 multiply_add_fusion
  10.3 2.6 convolution_convert_fusion.1
  12.9 4.9 %reshape.44 = bf16[32,6,8192]{2,1,0:T(8,128)(2,1)} reshape(bf16[192,8192]{1,0:T(8,128)(2,1)} %convolution_convert_fusion.1) | data formatting | bytes 6291456 | tf_op jit(solution)/shard_map/reshape | solution.py:54
  17.8 10.4 %all-to-all-start = ((bf16[32,6,8192]{2,1,0:T(8,128)(2,1)}), bf16[32,6,8192]{2,1,0:T(8,128)(2,1)}, u32[]{:S(2)}, u32[]{:S(2)}) async-start(bf16[32,6,8192]{2,1,0:T(8,128)(2,1)} %reshape.44), calls=%async_computation | async-start | bytes 8388608 | tf_op jit(solution)/shard_map/all_to_all | solution.py:56
  28.3 0.0 all-gather.5.cloned.1.call-start
  28.3 0.7 all-gather.5.cloned.1.call-update
  29.0 0.0 all-reduce.3.cloned.1.call-start
  29.1 50.0 %all-to-all-done = bf16[32,6,8192]{2,1,0:T(8,128)(2,1)} async-done(((bf16[32,6,8192]{2,1,0:T(8,128)(2,1)}), bf16[32,6,8192]{2,1,0:T(8,128)(2,1)}, u32[]{:S(2)}, u32[]{:S(2)}) %all-to-all-start) | async-done | bytes 3145760 | tf_op jit(solution)/shard_map/all_to_all | solution.py:56
  79.1 4.9 %reshape.45 = bf16[192,8192]{1,0:T(8,128)(2,1)} reshape(bf16[32,6,8192]{2,1,0:T(8,128)(2,1)} %all-to-all-done) | data formatting | bytes 6291456 | tf_op jit(solution)/shard_map/reshape | solution.py:58
  84.0 1.3 all-gather.3.cloned.1.call-done
  85.3 3.3 convolution_convert_fusion.2
  88.6 66.5 %all-gather.5.cloned.1.call-done = bf16[1,64,8192]{2,1,0:T(8,128)(2,1)} async-done(((bf16[1,64,512]{2,1,0:T(8,128)(2,1)}), bf16[1,64,8192]{2,1,0:T(8,128)(2,1)}) %all-gather.5.cloned.1.call-update) | async-done | bytes 1048592 | tf_op jit(solution)/shard_map/all_gather | solution.py:48
  155.0 3.9 fusion
  158.9 4.9 %reshape.46 = bf16[32,6,8192]{2,1,0:T(8,128)(2,1)} reshape(bf16[192,8192]{1,0:T(8,128)(2,1)} %fusion) | data formatting | bytes 6291456 | tf_op jit(solution)/shard_map/reshape | solution.py:67
  163.8 56.6 %all_to_all.15 = bf16[32,6,8192]{2,1,0:T(8,128)(2,1)} all-to-all(bf16[32,6,8192]{2,1,0:T(8,128)(2,1)} %reshape.46), channel_id=1, replica_groups=mesh['dp'=16,'owner'=32] {'owner'}, dimensions={0} | all-to-all | bytes 6291456 | tf_op jit(solution)/shard_map/all_to_all | solution.py:66
  220.4 4.9 %reshape.47 = bf16[192,8192]{1,0:T(8,128)(2,1)} reshape(bf16[32,6,8192]{2,1,0:T(8,128)(2,1)} %all_to_all.15) | data formatting | bytes 6291456 | tf_op jit(solution)/shard_map/reshape | solution.py:73
  225.2 3.9 fusion.1
  229.1 2.6 convolution_convert_fusion
  231.7 4.9 %reshape.48 = bf16[32,6,8192]{2,1,0:T(8,128)(2,1)} reshape(bf16[192,8192]{1,0:T(8,128)(2,1)} %convolution_convert_fusion) | data formatting | bytes 6291456 | tf_op jit(solution)/shard_map/reshape | solution.py:54
  236.6 55.2 %all_to_all.16 = bf16[32,6,8192]{2,1,0:T(8,128)(2,1)} all-to-all(bf16[32,6,8192]{2,1,0:T(8,128)(2,1)} %reshape.48), channel_id=1, replica_groups=mesh['dp'=16,'owner'=32] {'owner'}, dimensions={0} | all-to-all | bytes 6291456 | tf_op jit(solution)/shard_map/all_to_all | solution.py:79
  291.8 4.9 %reshape.49 = bf16[192,8192]{1,0:T(8,128)(2,1)} reshape(bf16[32,6,8192]{2,1,0:T(8,128)(2,1)} %all_to_all.16) | data formatting | bytes 6291456 | tf_op jit(solution)/shard_map/reshape | solution.py:82
  296.7 4.0 convolution_multiply_fusion.1
  300.7 6.5 %fusion.4 = f32[64,8192]{1,0:T(8,128)} fusion(bf16[192,8192]{1,0:T(8,128)(2,1)} %reshape.45, bf16[192,8192]{1,0:T(8,128)(2,1)} %reshape.49, bf16[1,64,8192]{2,1,0:T(8,128)(2,1)S(1)} %copy-done.1), kind=kOutput, calls=%fused_computation.12 | convolution fusion | flops 402677760 | bytes 9437184 | tf_op jit(solution)/shard_map/dot_general | solution.py:95
  307.2 0.0 all-reduce.3.cloned.1.call-update
  307.3 0.5 broadcast_multiply_fusion
  307.8 151.6 %all-reduce.3.cloned.1.call-done = (f32[64,8192]{1,0:T(8,128)}, f32[64,8192]{1,0:T(8,128)}) async-done(((f32[64,8192]{1,0:T(8,128)}, f32[64,8192]{1,0:T(8,128)}), (f32[64,8192]{1,0:T(8,128)}, f32[64,8192]{1,0:T(8,128)})) %all-reduce.3.cloned.1.call-update) | async-done | bytes 4194320 | tf_op jit(solution)/shard_map/psum | solution.py:98
  459.4 1.8 fusion.13
  (12 shorter events, 0.0 us)
Async XLA Ops:
  7.2 3.2 copy-start
  7.2 78.1 %all-gather.3.cloned.1.call-start = ((), (), s32[]{:S(2)}) async-start(), calls=%async_computation.3 | async-start | bytes 1114112 | tf_op jit(solution)/shard_map/all_gather | solution.py:47
  17.8 61.2 %all-to-all-start = ((bf16[32,6,8192]{2,1,0:T(8,128)(2,1)}), bf16[32,6,8192]{2,1,0:T(8,128)(2,1)}, u32[]{:S(2)}, u32[]{:S(2)}) async-start(bf16[32,6,8192]{2,1,0:T(8,128)(2,1)} %reshape.44), calls=%async_computation | async-start | bytes 8388608 | tf_op jit(solution)/shard_map/all_to_all | solution.py:56
  28.3 126.8 %all-gather.5.cloned.1.call-start = ((), (), s32[]{:S(2)}) async-start(), calls=%async_computation.4 | async-start | bytes 1114112 | tf_op jit(solution)/shard_map/all_gather | solution.py:48
  29.0 430.4 %all-reduce.3.cloned.1.call-start = ((), (), s32[]{:S(2)}) async-start(), calls=%async_computation.5 | async-start | bytes 8388608 | tf_op jit(solution)/shard_map/psum | solution.py:98
  296.7 4.0 copy-start.1
  307.2 152.2 %copy-start.2 = (bf16[1,64,512]{2,1,0:T(8,128)(2,1)S(1)}, bf16[1,64,512]{2,1,0:T(8,128)(2,1)}, u32[]{:S(2)}) copy-start(bf16[1,64,512]{2,1,0:T(8,128)(2,1)} %param.15) | copy-start | bytes 196612
  307.2 152.2 %copy-start.3 = (bf16[1,64,512]{2,1,0:T(8,128)(2,1)S(1)}, bf16[1,64,512]{2,1,0:T(8,128)(2,1)}, u32[]{:S(2)}) copy-start(bf16[1,64,512]{2,1,0:T(8,128)(2,1)} %param.14) | copy-start | bytes 196612
  307.2 152.2 %copy-start.4 = (bf16[1,64,512]{2,1,0:T(8,128)(2,1)S(1)}, bf16[1,64,512]{2,1,0:T(8,128)(2,1)}, u32[]{:S(2)}) copy-start(bf16[1,64,512]{2,1,0:T(8,128)(2,1)} %param.17) | copy-start | bytes 196612
  307.2 152.2 %copy-start.5 = (bf16[1,64,512]{2,1,0:T(8,128)(2,1)S(1)}, bf16[1,64,512]{2,1,0:T(8,128)(2,1)}, u32[]{:S(2)}) copy-start(bf16[1,64,512]{2,1,0:T(8,128)(2,1)} %param.16) | copy-start | bytes 196612
Sparse Core Ops, SparseCore 0:
  10.1 75.1 all-gather.2
  87.4 67.6 all-gather.4
  307.4 151.9 all-reduce.2
where the time goes:
time: 469 us; the launch traced here: 468 us
  waiting for transfers between devices  271 us (58%)
  blocking collectives  112 us (24%)
  local copies, waits for them, and re-layouts  29.4 us (6%)
  matrix products  26.8 us (6%)
  between operations  13.8 us (3%)
  starting transfers between devices  10.5 us (2%)
  other arithmetic  4.76 us (1%)
    psum x1, waiting for transfers between devices, body(): summed_down, summed_up = lax.psum((down_grad, up_gradient), 'dp')  152 us
    all_gather x1, waiting for transfers between devices, body(): lax.all_gather(adapter_up_weight, 'dp', axis=2, tiled=True)  66.5 us
    all_to_all x1, blocking collectives, body(): lax.all_to_all(adapter_output.reshape(owner_index, slot_capacity, model_w...  56.6 us
    all_to_all x1, blocking collectives, body(): lax.all_to_all(spread(shifted_index.astype(jnp.bfloat16)), 'owner', split...  55.2 us
    all_to_all x1, waiting for transfers between devices, body(): lax.all_to_all(spread(tokens), 'owner', split_axis=0, concat_axis=0, tile...  50 us
    all_to_all x1, starting transfers between devices, body(): lax.all_to_all(spread(tokens), 'owner', split_axis=0, concat_axis=0, tile...  10.4 us
    reshape x2, local copies, waits for them, and re-layouts, spread(): placed_rows(row_block)  9.78 us
  transfers between devices with their start and end apart: 4, of which 4 were waited for; matrix products, arithmetic and copies ran while one was open for 4% of the time, Pallas kernels for 0%

commit v1 on v0

--- a/solution.py
+++ b/solution.py
@@ -5,6 +5,11 @@
 
 adapter_scale = 0.5
 adam_eps = 1e-08
+
+
+def all_by_exchange(x, axis, dim):
+    sent = jnp.stack([x] * lax.axis_size(axis))
+    return jnp.concatenate(lax.all_to_all(sent, axis, 0, 0), axis=dim)
 
 
 def adam_update(grad, first, second):
@@ -45,7 +50,7 @@
 
     down_full, up_weight_whole = (
         lax.all_gather(adapter_down_weight, "dp", axis=2, tiled=True),
-        lax.all_gather(adapter_up_weight, "dp", axis=2, tiled=True),
+        all_by_exchange(adapter_up_weight, "dp", 2),
     )
     down_full = down_full[0]
     up_weight_whole = up_weight_whole[0]

time: 469 us -> 493 us (1.051)
  blocking collectives: 112 us -> 170 us
  waiting for transfers between devices: 271 us -> 231 us
    all_gather x1, waiting for transfers between devices: 1.28 us -> 79.4 us  [body(): lax.all_gather(adapter_down_weight, 'dp', axis=2, tiled=True)]
    all_gather x1 -> x0, waiting for transfers between devices: 66.5 us -> none  [body(): lax.all_gather(adapter_up_weight, 'dp', axis=2, tiled=True)]
    all_to_all x0 -> x1, blocking collectives: none -> 59.5 us  [body(): lax.all_to_all(spread(tokens), 'owner', split_axis=0, concat_axis=0, tile...]
    all_to_all x1, waiting for transfers between devices: 50 us -> 0.01 us  [all_by_exchange(): return jnp.concatenate(lax.all_to_all(sent, axis, 0, 0), axis=dim)]
  transfers between devices with their start and end apart: 4 -> 3, of which waited for: 4 -> 2; matrix products, arithmetic and copies ran while one was open for 4% -> 2% of each run, Pallas kernels for 0% -> 0%
where the time goes in v1:
time: 493 us; the launch traced here: 492 us
  waiting for transfers between devices  231 us (47%)
  blocking collectives  170 us (34%)
  local copies, waits for them, and re-layouts  32.7 us (7%)
  matrix products  25.6 us (5%)
  between operations  14.1 us (3%)
  starting transfers between devices  12.6 us (3%)
    psum x1, waiting for transfers between devices, body(): summed_down, summed_up = lax.psum((down_grad, up_gradient), 'dp')  151 us
    all_gather x1, waiting for transfers between devices, body(): lax.all_gather(adapter_down_weight, 'dp', axis=2, tiled=True)  79.4 us
    all_to_all x1, blocking collectives, body(): lax.all_to_all(spread(tokens), 'owner', split_axis=0, concat_axis=0, tile...  59.5 us
    all_to_all x1, blocking collectives, body(): lax.all_to_all(adapter_output.reshape(owner_index, slot_capacity, model_w...  55.5 us
    all_to_all x1, blocking collectives, body(): lax.all_to_all(spread(shifted_index.astype(jnp.bfloat16)), 'owner', split...  55.2 us
    all_to_all x1, starting transfers between devices, all_by_exchange(): return jnp.concatenate(lax.all_to_all(sent, axis, 0, 0), axis=dim)  12.5 us
  transfers between devices with their start and end apart: 3, of which 2 were waited for; matrix products, arithmetic and copies ran while one was open for 2% of the time, Pallas kernels for 0%

profile of v1, /device:TPU:6, one launch (start us, length us, event | category | flops | bytes accessed | tf_op | source)
XLA Modules:
  0.0 491.6 jit_solution(5974878436663460717)
XLA Ops:
  7.2 0.9 fusion.16
  8.1 0.2 reduce_window_sum.11
  8.2 0.8 select_reduce_fusion
  9.1 0.7 multiply_add_fusion
  9.7 2.6 convolution_convert_fusion.1
  12.4 4.9 reshape.50
  17.2 59.5 %all_to_all.20 = bf16[32,6,8192]{2,1,0:T(8,128)(2,1)} all-to-all(bf16[32,6,8192]{2,1,0:T(8,128)(2,1)} %reshape.50), channel_id=1, replica_groups=mesh['dp'=16,'owner'=32] {'owner'}, dimensions={0} | all-to-all | bytes 6291456 | tf_op jit(solution)/shard_map/all_to_all | solution.py:61
  76.7 1.1 stack.2
  77.8 12.5 %all-to-all-start.1 = ((bf16[16,1,64,512]{3,2,1,0:T(8,128)(2,1)}), bf16[16,1,64,512]{3,2,1,0:T(8,128)(2,1)S(1)}, u32[]{:S(2)}, u32[]{:S(2)}) async-start(bf16[16,1,64,512]{3,2,1,0:T(8,128)(2,1)} %stack.2), calls=%async_computation.1 | async-start | bytes 2097152 | tf_op jit(solution)/shard_map/all_to_all | solution.py:12
  90.4 0.0 all-gather.2.cloned.1.call-start
  90.4 0.7 all-gather.2.cloned.1.call-update
  91.1 0.0 all-reduce.3.cloned.1.call-start
  91.2 5.0 %reshape.51 = bf16[192,8192]{1,0:T(8,128)(2,1)} reshape(bf16[32,6,8192]{2,1,0:T(8,128)(2,1)} %all_to_all.20) | data formatting | bytes 6291456 | tf_op jit(solution)/shard_map/reshape | solution.py:63
  96.1 79.4 %all-gather.2.cloned.1.call-done = bf16[1,64,8192]{2,1,0:T(8,128)(2,1)} async-done(((bf16[1,64,512]{2,1,0:T(8,128)(2,1)}), bf16[1,64,8192]{2,1,0:T(8,128)(2,1)}) %all-gather.2.cloned.1.call-update) | async-done | bytes 1048592 | tf_op jit(solution)/shard_map/all_gather | solution.py:52
  175.5 3.3 convolution_convert_fusion.2
  178.8 1.0 copy-done.1
  179.7 1.3 copy.13
  181.1 2.7 fusion
  183.7 4.9 reshape.53
  188.6 55.5 %all_to_all.21 = bf16[32,6,8192]{2,1,0:T(8,128)(2,1)} all-to-all(bf16[32,6,8192]{2,1,0:T(8,128)(2,1)} %reshape.53), channel_id=1, replica_groups=mesh['dp'=16,'owner'=32] {'owner'}, dimensions={0} | all-to-all | bytes 6291456 | tf_op jit(solution)/shard_map/all_to_all | solution.py:71
  244.1 4.9 reshape.54
  249.0 3.9 fusion.1
  252.8 2.6 convolution_convert_fusion
  255.5 4.9 reshape.55
  260.3 55.2 %all_to_all.22 = bf16[32,6,8192]{2,1,0:T(8,128)(2,1)} all-to-all(bf16[32,6,8192]{2,1,0:T(8,128)(2,1)} %reshape.55), channel_id=1, replica_groups=mesh['dp'=16,'owner'=32] {'owner'}, dimensions={0} | all-to-all | bytes 6291456 | tf_op jit(solution)/shard_map/all_to_all | solution.py:84
  315.5 4.9 reshape.56
  320.4 4.0 convolution_multiply_fusion.1
  324.4 6.6 %fusion.4 = f32[64,8192]{1,0:T(8,128)} fusion(bf16[192,8192]{1,0:T(8,128)(2,1)} %reshape.51, bf16[192,8192]{1,0:T(8,128)(2,1)} %reshape.56, bf16[64,8192]{1,0:T(8,128)(2,1)S(1)} %bitcast.40), kind=kOutput, calls=%fused_computation.12 | convolution fusion | flops 402677760 | bytes 9437184 | tf_op jit(solution)/shard_map/dot_general | solution.py:100
  330.9 0.0 all-reduce.3.cloned.1.call-update
  331.0 0.5 broadcast_multiply_fusion
  331.5 151.4 %all-reduce.3.cloned.1.call-done = (f32[64,8192]{1,0:T(8,128)}, f32[64,8192]{1,0:T(8,128)}) async-done(((f32[64,8192]{1,0:T(8,128)}, f32[64,8192]{1,0:T(8,128)}), (f32[64,8192]{1,0:T(8,128)}, f32[64,8192]{1,0:T(8,128)})) %all-reduce.3.cloned.1.call-update) | async-done | bytes 4194320 | tf_op jit(solution)/shard_map/psum | solution.py:103
  482.9 1.8 fusion.10
  (14 shorter events, 0.0 us)
Async XLA Ops:
  7.2 2.6 copy-start
  17.2 59.5 %copy-start.2 = (bf16[1,64,512]{2,1,0:T(8,128)(2,1)S(1)}, bf16[1,64,512]{2,1,0:T(8,128)(2,1)}, u32[]{:S(2)}) copy-start(bf16[1,64,512]{2,1,0:T(8,128)(2,1)} %param.13) | copy-start | bytes 196612
  77.8 100.9 %all-to-all-start.1 = ((bf16[16,1,64,512]{3,2,1,0:T(8,128)(2,1)}), bf16[16,1,64,512]{3,2,1,0:T(8,128)(2,1)S(1)}, u32[]{:S(2)}, u32[]{:S(2)}) async-start(bf16[16,1,64,512]{3,2,1,0:T(8,128)(2,1)} %stack.2), calls=%async_computation.1 | async-start | bytes 2097152 | tf_op jit(solution)/shard_map/all_to_all | solution.py:12
  90.4 85.1 %all-gather.2.cloned.1.call-start = ((), (), s32[]{:S(2)}) async-start(), calls=%async_computation.4 | async-start | bytes 1114112 | tf_op jit(solution)/shard_map/all_gather | solution.py:52
  91.1 391.8 %all-reduce.3.cloned.1.call-start = ((), (), s32[]{:S(2)}) async-start(), calls=%async_computation.5 | async-start | bytes 8388608 | tf_op jit(solution)/shard_map/psum | solution.py:103
  178.8 1.0 copy-start.1
  330.9 152.0 %copy-start.3 = (bf16[1,64,512]{2,1,0:T(8,128)(2,1)S(1)}, bf16[1,64,512]{2,1,0:T(8,128)(2,1)}, u32[]{:S(2)}) copy-start(bf16[1,64,512]{2,1,0:T(8,128)(2,1)} %param.15) | copy-start | bytes 196612
  330.9 152.0 %copy-start.4 = (bf16[1,64,512]{2,1,0:T(8,128)(2,1)S(1)}, bf16[1,64,512]{2,1,0:T(8,128)(2,1)}, u32[]{:S(2)}) copy-start(bf16[1,64,512]{2,1,0:T(8,128)(2,1)} %param.14) | copy-start | bytes 196612
  330.9 152.0 %copy-start.5 = (bf16[1,64,512]{2,1,0:T(8,128)(2,1)S(1)}, bf16[1,64,512]{2,1,0:T(8,128)(2,1)}, u32[]{:S(2)}) copy-start(bf16[1,64,512]{2,1,0:T(8,128)(2,1)} %param.17) | copy-start | bytes 196612
  330.9 152.0 %copy-start.6 = (bf16[1,64,512]{2,1,0:T(8,128)(2,1)S(1)}, bf16[1,64,512]{2,1,0:T(8,128)(2,1)}, u32[]{:S(2)}) copy-start(bf16[1,64,512]{2,1,0:T(8,128)(2,1)} %param.16) | copy-start | bytes 196612
Sparse Core Ops, SparseCore 0:
  93.3 82.1 all-gather.1
  331.1 151.7 all-reduce.2
